TPU v7x, 512 devices: a whole 4x4x16 slice. The times are simulated.
512 devices in a mesh: dp: 8 (over x, core), expert: 64 (over y, z).
Axes of the slice: x: 4, y: 4, z: 16, core: 2. Of those that a mesh axis runs over, the one named last changes fastest.
Arguments:
- query_rows: bfloat16 [65536, 2048], P(('dp', 'expert')), may hold values from -40 to 40
- key_rows: bfloat16 [65536, 256], P(('dp', 'expert')), may hold values from -40 to 40
- value_rows: bfloat16 [65536, 256], P(('dp', 'expert')), may hold values from -6 to 6
- residual: bfloat16 [65536, 1024], P(('dp', 'expert')), may hold values from -25 to 25
- document_owner: int32 [512, 8], P(('dp', 'expert')), may hold values from 0 to 7, as said below
- document_length: int32 [512, 8], P(('dp', 'expert')), may hold values from 8 to 24, as said below
- document_offset: int32 [512, 8], P(('dp', 'expert')), may hold values from 0 to 120, as said below
- query_gain: float32 [128], replicated, may hold values from 0.3 to 5.5
- key_gain: float32 [128], replicated, may hold values from 0.3 to 5.5
- output_weight: bfloat16 [2048, 1024], P('expert'), may hold values from -0.125 to 0.125
- post_gain: float32 [1024], replicated, may hold values from 0.5 to 2
- routes: int32 [65536, 8], P(('dp', 'expert')), may hold values from 0 to 63, all different within a row; in each aligned block of 128 rows (0 to 127, 128 to 255, ...) at most 20 rows name the same one
- route_weight: float32 [65536, 8], P(('dp', 'expert')), may hold values from 0.1 to 1
- gate_weight: bfloat16 [64, 768, 1024], P('expert', 'dp'), may hold values from -0.1875 to 0.1875
- up_weight: bfloat16 [64, 768, 1024], P('expert', 'dp'), may hold values from -0.1875 to 0.1875
- down_weight: bfloat16 [64, 768, 1024], P('expert', 'dp'), may hold values from -0.21875 to 0.21875
Outputs:
- layer_out: bfloat16 [65536, 1024], P(('dp', 'expert'))
Inputs may be any that keep to these rules, and one draw needn't show every extreme that they name: `document_owner`: each device's row names every dp index once, so a device sends exactly one document to each pack owner of its expert column. `document_length`: A device's lengths sum to 128; the documents that all devices of an expert column send to one owner also sum to 128; no device sends more than 24 rows to one owner, and some device does in every column. `document_offset`: the documents that reach one owner cover its 128 pack rows exactly once. `routes`: at most 20 of one device's rows name one expert; a row names 8 different experts.
All inputs are finite; a program needn't handle non-finite values.
Results may differ from a plain program's by a relative error of at most 0.012.
The roundings to bfloat16 on the way count: a program that leaves them out, or rounds other values in their place, can miss the bound.
Values may be sent and summed in bfloat16 or wider, within the bound.
No kernel may reach another device: no remote copies, remote signals or barrier semaphores. Data moves between devices by JAX's collectives and lax.ppermute only.
A program may use at most 64 MiB of HBM per device.

v0:
```python
import jax
import jax.numpy as jnp
from jax import lax
from jax.sharding import PartitionSpec as P

norm_epsilon = 1e-06
rope_base = 1000000.0


def rms_scale(values, gain):
    mean_square = jnp.mean(values * values, axis=-1, keepdims=True)
    return values * lax.rsqrt(mean_square + norm_epsilon) * gain


def rotary(values, positions):
    head_width = values.shape[-1]
    half_width = head_width // 2
    frequency = rope_base ** (-2.0 * jnp.arange(half_width, dtype=jnp.float32) / head_width)
    angles = positions.astype(jnp.float32)[:, None] * frequency[None, :]
    cosine_part = jnp.cos(angles)[:, None, :]
    sine_part = jnp.sin(angles)[:, None, :]
    leading = values[..., :half_width]
    trailing = values[..., half_width:]
    return jnp.concatenate(
        [
            leading * cosine_part - trailing * sine_part,
            trailing * cosine_part + leading * sine_part,
        ],
        axis=-1,
    )


def attend(query_part, key_part, value_part, identity, position, query_gain, key_gain):
    row_total = query_part.shape[0]
    head_width = query_gain.shape[0]
    head_count = query_part.shape[1] // head_width
    key_heads = key_part.shape[1] // head_width
    group_size = head_count // key_heads
    queries = rotary(
        rms_scale(
            query_part.reshape(row_total, head_count, head_width).astype(jnp.float32), query_gain
        ),
        position,
    ).astype(jnp.bfloat16)
    keys_normed = rotary(
        rms_scale(key_part.reshape(row_total, key_heads, head_width).astype(jnp.float32), key_gain),
        position,
    ).astype(jnp.bfloat16)
    queries = queries.reshape(row_total, key_heads, group_size, head_width)
    scores = jnp.einsum(
        "pkgd,qkd->kgpq", queries, keys_normed, preferred_element_type=jnp.float32
    ) * head_width ** (-0.5)
    allowed = (identity[:, None] == identity[None, :]) & (position[None, :] <= position[:, None])
    scores = jnp.where(allowed, scores, -jnp.inf)
    largest = jnp.max(scores, axis=-1, keepdims=True)
    powers = jnp.exp(scores - largest)
    weights = (powers / jnp.sum(powers, axis=-1, keepdims=True)).astype(jnp.bfloat16)
    values_heads = value_part.reshape(row_total, key_heads, head_width)
    mixed = jnp.einsum("kgpq,qkd->pkgd", weights, values_heads, preferred_element_type=jnp.float32)
    return mixed.astype(jnp.bfloat16).reshape(row_total, head_count * head_width)


def project_heads(attended, output_weight):
    return jnp.dot(
        attended,
        lax.all_gather(output_weight, "expert", axis=0, tiled=True),
        preferred_element_type=jnp.float32,
    )


def hidden_product(block, gate_part, up_part, down_part):
    contract = (((1,), (1,)), ((), ()))
    gate_value = lax.dot_general(block, gate_part, contract, preferred_element_type=jnp.float32)
    up_value = lax.dot_general(block, up_part, contract, preferred_element_type=jnp.float32)
    active = (jax.nn.silu(gate_value) * up_value).astype(jnp.bfloat16)
    return jnp.dot(active, down_part, preferred_element_type=jnp.float32)


def expert_output(work_rows, gate_part, up_part, down_part):
    return hidden_product(work_rows, gate_part, up_part, down_part)


def local(
    query_rows,
    key_rows,
    value_rows,
    residual,
    document_owner,
    document_length,
    document_offset,
    query_gain,
    key_gain,
    output_weight,
    post_gain,
    routes,
    route_weight,
    gate_weight,
    up_weight,
    down_weight,
):
    owner_total = lax.axis_size("dp")
    expert_total = lax.axis_size("expert")
    row_total = query_rows.shape[0]
    capacity = row_total * 3 // (2 * owner_total)
    owners = document_owner[0]
    lengths = document_length[0]
    offsets = document_offset[0]
    starts = jnp.cumsum(lengths) - lengths
    owner_ids = jnp.arange(owner_total, dtype=jnp.int32)
    matches = owners[None, :] == owner_ids[:, None]
    start_of = jnp.sum(jnp.where(matches, starts[None, :], 0), axis=1)
    length_of = jnp.sum(jnp.where(matches, lengths[None, :], 0), axis=1)
    offset_of = jnp.sum(jnp.where(matches, offsets[None, :], 0), axis=1)
    slot_ids = jnp.arange(capacity, dtype=jnp.int32)
    source_rows = jnp.minimum(start_of[:, None] + slot_ids[None, :], row_total - 1).reshape(-1)
    pack_slot = jnp.where(
        slot_ids[None, :] < length_of[:, None], offset_of[:, None] + slot_ids[None, :], -1
    )
    total_slots = owner_total * capacity
    flat_slots = jnp.arange(total_slots, dtype=jnp.int32)
    pack_ids = jnp.arange(row_total, dtype=jnp.int32)
    got_query, got_key, got_value, got_residual, got_slot = (
        lax.all_to_all(
            query_rows[source_rows].reshape(owner_total, capacity, -1),
            "dp",
            split_axis=0,
            concat_axis=0,
            tiled=True,
        ),
        lax.all_to_all(
            key_rows[source_rows].reshape(owner_total, capacity, -1),
            "dp",
            split_axis=0,
            concat_axis=0,
            tiled=True,
        ),
        lax.all_to_all(
            value_rows[source_rows].reshape(owner_total, capacity, -1),
            "dp",
            split_axis=0,
            concat_axis=0,
            tiled=True,
        ),
        lax.all_to_all(
            residual[source_rows].reshape(owner_total, capacity, -1),
            "dp",
            split_axis=0,
            concat_axis=0,
            tiled=True,
        ),
        lax.all_to_all(pack_slot, "dp", split_axis=0, concat_axis=0, tiled=True),
    )
    placed = got_slot.reshape(-1)[None, :] == pack_ids[:, None]
    slot_of = jnp.sum(jnp.where(placed, flat_slots[None, :], 0), axis=1)
    pack_query = got_query.reshape(total_slots, -1)[slot_of]
    pack_key = got_key.reshape(total_slots, -1)[slot_of]
    pack_value = got_value.reshape(total_slots, -1)[slot_of]
    pack_residual = got_residual.reshape(total_slots, -1)[slot_of]
    identity = slot_of // capacity
    position = slot_of % capacity
    attended = attend(pack_query, pack_key, pack_value, identity, position, query_gain, key_gain)
    hidden_state = pack_residual.astype(jnp.float32) + project_heads(attended, output_weight)
    normed = rms_scale(hidden_state, post_gain).astype(jnp.bfloat16)
    top_total = routes.shape[1]
    most = row_total * top_total * 5 // (4 * expert_total)
    expert_ids = jnp.arange(expert_total, dtype=jnp.int32)
    routed = routes[:, :, None] == expert_ids[None, None, :]
    chosen = jnp.sum(routed.astype(jnp.int32), axis=1)
    earlier = (pack_ids[None, :] < pack_ids[:, None]).astype(jnp.int32)
    rank = jnp.dot(earlier, chosen)
    ranked = jnp.where(chosen > 0, rank, -1)
    place_ids = jnp.arange(most, dtype=jnp.int32)
    hits = ranked.T[:, :, None] == place_ids[None, None, :]
    source_token = jnp.sum(jnp.where(hits, pack_ids[None, :, None], 0), axis=1)
    outgoing = normed[source_token.reshape(-1)].reshape(expert_total, most, -1)
    total_rows = expert_total * most
    received = lax.all_to_all(outgoing, "expert", split_axis=0, concat_axis=0, tiled=True)
    work_rows = received.reshape(total_rows, -1)
    gate_whole, up_whole, down_whole = (
        lax.all_gather(gate_weight, "dp", axis=1, tiled=True),
        lax.all_gather(up_weight, "dp", axis=1, tiled=True),
        lax.all_gather(down_weight, "dp", axis=1, tiled=True),
    )
    produced = expert_output(work_rows, gate_whole[0], up_whole[0], down_whole[0])
    produced = produced.astype(jnp.bfloat16)
    out_slots = produced.reshape(expert_total, most, -1)
    returned = lax.all_to_all(out_slots, "expert", split_axis=0, concat_axis=0, tiled=True)
    flat_back = returned.reshape(total_rows, -1)
    copy_rank = jnp.sum(jnp.where(routed, rank[:, None, :], 0), axis=2)
    copy_index = routes * most + copy_rank
    gates = route_weight / jnp.sum(route_weight, axis=1, keepdims=True)
    mixture = jnp.zeros(hidden_state.shape, jnp.float32)
    for route_slot in range(top_total):
        mixture = mixture + gates[:, route_slot : route_slot + 1] * flat_back[
            copy_index[:, route_slot]
        ].astype(jnp.float32)
    return (hidden_state + mixture).astype(jnp.bfloat16)


def solution(mesh):
    placed = (
        P(("dp", "expert"), None),
        P(("dp", "expert"), None),
        P(("dp", "expert"), None),
        P(("dp", "expert"), None),
        P(("dp", "expert"), None),
        P(("dp", "expert"), None),
        P(("dp", "expert"), None),
        P(),
        P(),
        P("expert", None),
        P(),
        P(("dp", "expert"), None),
        P(("dp", "expert"), None),
        P("expert", "dp", None),
        P("expert", "dp", None),
        P("expert", "dp", None),
    )
    return jax.shard_map(
        local, mesh=mesh, in_specs=placed, out_specs=P(("dp", "expert"), None), check_vma=False
    )
```

profile of v0, /device:TPU:32, one launch (start us, length us, event | category | flops | bytes accessed | tf_op | source)
XLA Modules:
  0.0 508.2 jit_solution(4077008279144218235)
XLA Ops:
  11.1 4.3 all-to-all-start.1
  18.4 2.0 gather_fusion.6
  25.5 4.9 all-to-all-start.3
  32.0 4.3 all-to-all-done.3
  36.2 3.4 all-to-all-start.2
  39.6 5.7 %all-to-all-done.2 = bf16[8,24,256]{2,1,0:T(8,128)(2,1)S(1)} async-done(((bf16[8,24,256]{2,1,0:T(8,128)(2,1)}), bf16[8,24,256]{2,1,0:T(8,128)(2,1)S(1)}, u32[]{:S(2)}, u32[]{:S(2)}) %all-to-all-start.2) | async-done | bytes 98336 | tf_op jit(solution)/shard_map/all_to_all | solution.py:137
  45.3 3.5 all-to-all-start
  51.8 5.8 %all-to-all-done = bf16[8,24,1024]{2,1,0:T(8,128)(2,1)S(1)} async-done(((bf16[8,24,1024]{2,1,0:T(8,128)(2,1)}), bf16[8,24,1024]{2,1,0:T(8,128)(2,1)S(1)}, u32[]{:S(2)}, u32[]{:S(2)}) %all-to-all-start) | async-done | bytes 393248 | tf_op jit(solution)/shard_map/all_to_all | solution.py:144
  57.6 3.5 all-to-all-start.4
  62.3 11.9 %all-to-all-done.4 = bf16[8,24,2048]{2,1,0:T(8,128)(2,1)S(1)} async-done(((bf16[8,24,2048]{2,1,0:T(8,128)(2,1)}), bf16[8,24,2048]{2,1,0:T(8,128)(2,1)S(1)}, u32[]{:S(2)}, u32[]{:S(2)}) %all-to-all-start.4) | async-done | bytes 786464 | tf_op jit(solution)/shard_map/all_to_all | solution.py:123
  79.7 81.6 %all-gather.5.cloned.1.call-done = bf16[2048,1024]{1,0:T(8,128)(2,1)} async-done(((bf16[32,1024]{1,0:T(8,128)(2,1)}), bf16[2048,1024]{1,0:T(8,128)(2,1)}) %all-gather.5.cloned.1.call-update) | async-done | bytes 4194320 | tf_op jit(solution)/shard_map/all_gather | solution.py:66
  161.3 3.0 multiply_reduce_fusion.1
  165.2 4.3 gather_fusion.8
  169.5 2.3 reshape.331
  171.9 9.3 %all-to-all-start.5 = ((bf16[64,20,1024]{2,1,0:T(8,128)(2,1)}), bf16[64,20,1024]{2,1,0:T(8,128)(2,1)}, u32[]{:S(2)}, u32[]{:S(2)}) async-start(bf16[64,20,1024]{2,1,0:T(8,128)(2,1)} %reshape.331), calls=%async_computation.5 | async-start | bytes 6291456 | tf_op jit(solution)/shard_map/all_to_all | solution.py:177
  182.9 131.6 %all-to-all-done.5 = bf16[64,20,1024]{2,1,0:T(8,128)(2,1)} async-done(((bf16[64,20,1024]{2,1,0:T(8,128)(2,1)}), bf16[64,20,1024]{2,1,0:T(8,128)(2,1)}, u32[]{:S(2)}, u32[]{:S(2)}) %all-to-all-start.5) | async-done | bytes 2621472 | tf_op jit(solution)/shard_map/all_to_all | solution.py:177
  314.6 3.6 reshape.332
  318.3 5.5 %fusion.4 = f32[1280,768]{1,0:T(8,128)} fusion(bf16[1280,1024]{1,0:T(8,128)(2,1)S(1)} %reshape.332, bf16[1,768,1024]{2,1,0:T(8,128)(2,1)} %all-gather.7.cloned.1.call-done), kind=kOutput, calls=%fused_computation.23 | convolution fusion | flops 2013265920 | bytes 8126464 | tf_op jit(solution)/shard_map/dot_general | solution.py:73
  323.8 10.0 %convolution_convert_fusion = bf16[1280,1024]{1,0:T(8,128)(2,1)} fusion(bf16[1,768,1024]{2,1,0:T(8,128)(2,1)} %all-gather.11.cloned.1.call-done, bf16[1280,1024]{1,0:T(8,128)(2,1)S(1)} %reshape.332, f32[1280,768]{1,0:T(8,128)} %fusion.4, bf16[1,768,1024]{2,1,0:T(8,128)(2,1)} %all-gather.9.cloned.1.call-done), kind=kOutput, calls=%fused_computation.19 | convolution fusion | flops 4033740800 | bytes 12320768 | tf_op jit(solution)/shard_map/dot_general | solution.py:76
  333.8 5.2 %reshape.333 = bf16[64,20,1024]{2,1,0:T(8,128)(2,1)} reshape(bf16[1280,1024]{1,0:T(8,128)(2,1)} %convolution_convert_fusion) | data formatting | bytes 5242880 | tf_op jit(solution)/shard_map/reshape | solution.py:186
  339.0 8.0 %all-to-all-start.6 = ((bf16[64,20,1024]{2,1,0:T(8,128)(2,1)}), bf16[64,20,1024]{2,1,0:T(8,128)(2,1)}, u32[]{:S(2)}, u32[]{:S(2)}) async-start(bf16[64,20,1024]{2,1,0:T(8,128)(2,1)} %reshape.333), calls=%async_computation.6 | async-start | bytes 6291456 | tf_op jit(solution)/shard_map/all_to_all | solution.py:187
  347.2 135.2 %all-to-all-done.6 = bf16[64,20,1024]{2,1,0:T(8,128)(2,1)} async-done(((bf16[64,20,1024]{2,1,0:T(8,128)(2,1)}), bf16[64,20,1024]{2,1,0:T(8,128)(2,1)}, u32[]{:S(2)}, u32[]{:S(2)}) %all-to-all-start.6) | async-done | bytes 2621472 | tf_op jit(solution)/shard_map/all_to_all | solution.py:187
  482.4 3.6 reshape.334
  497.9 2.8 add_convert_fusion.1
  (117 shorter events, 37.1 us)
Async XLA Ops:
  7.4 11.0 %copy-start = (bf16[128,2048]{1,0:T(8,128)(2,1)S(1)}, bf16[128,2048]{1,0:T(8,128)(2,1)}, u32[]{:S(2)}) copy-start(bf16[128,2048]{1,0:T(8,128)(2,1)} %param.16) | copy-start | bytes 1572868
  7.4 153.9 %all-gather.5.cloned.1.call-start = ((), (), s32[]{:S(2)}) async-start(), calls=%async_computation.7 | async-start | bytes 4259840 | tf_op jit(solution)/shard_map/all_gather | solution.py:66
  11.1 14.4 %all-to-all-start.1 = ((s32[8,1,24]{2,1,0:T(1,128)}), s32[8,1,24]{2,1,0:T(1,128)S(1)}, u32[]{:S(2)}, u32[]{:S(2)}) async-start(s32[8,1,24]{2,1,0:T(1,128)} %compare_select_fusion.1), calls=%async_computation.1 | async-start | bytes 8192 | tf_op jit(solution)/shard_map/all_to_all | solution.py:151
  18.4 2.0 copy-start.2
  18.4 3.7 copy-start.3
  20.4 3.3 copy-start.1
  25.5 35.7 %copy-start.14 = (f32[128]{0:T(128)S(1)}, f32[128]{0:T(128)}, u32[]{:S(2)}) copy-start(f32[128]{0:T(128)} %param.24) | copy-start | bytes 1540
  25.5 10.7 %all-to-all-start.3 = ((bf16[8,24,256]{2,1,0:T(8,128)(2,1)}), bf16[8,24,256]{2,1,0:T(8,128)(2,1)S(1)}, u32[]{:S(2)}, u32[]{:S(2)}) async-start(bf16[8,24,256]{2,1,0:T(8,128)(2,1)} %bitcast.14), calls=%async_computation.3 | async-start | bytes 196608 | tf_op jit(solution)/shard_map/all_to_all | solution.py:130
  36.2 9.1 %all-to-all-start.2 = ((bf16[8,24,256]{2,1,0:T(8,128)(2,1)}), bf16[8,24,256]{2,1,0:T(8,128)(2,1)S(1)}, u32[]{:S(2)}, u32[]{:S(2)}) async-start(bf16[8,24,256]{2,1,0:T(8,128)(2,1)} %bitcast.9), calls=%async_computation.2 | async-start | bytes 196608 | tf_op jit(solution)/shard_map/all_to_all | solution.py:137
  45.3 12.3 %all-to-all-start = ((bf16[8,24,1024]{2,1,0:T(8,128)(2,1)}), bf16[8,24,1024]{2,1,0:T(8,128)(2,1)S(1)}, u32[]{:S(2)}, u32[]{:S(2)}) async-start(bf16[8,24,1024]{2,1,0:T(8,128)(2,1)} %bitcast.3), calls=%async_computation | async-start | bytes 786432 | tf_op jit(solution)/shard_map/all_to_all | solution.py:144
  57.6 16.6 %all-to-all-start.4 = ((bf16[8,24,2048]{2,1,0:T(8,128)(2,1)}), bf16[8,24,2048]{2,1,0:T(8,128)(2,1)S(1)}, u32[]{:S(2)}, u32[]{:S(2)}) async-start(bf16[8,24,2048]{2,1,0:T(8,128)(2,1)} %bitcast.19), calls=%async_computation.4 | async-start | bytes 1572864 | tf_op jit(solution)/shard_map/all_to_all | solution.py:123
  61.4 15.8 %copy-start.7 = (bf16[128,2,64]{2,0,1:T(8,128)(2,1)}, bf16[128,2,64]{2,0,1:T(8,128)(2,1)S(1)}, u32[]{:S(2)}) copy-start(bf16[128,2,64]{2,0,1:T(8,128)(2,1)S(1)} %get-tuple-element.12) | copy-start | bytes 98308
  61.4 15.8 %copy-start.8 = (bf16[128,2,64]{2,0,1:T(8,128)(2,1)}, bf16[128,2,64]{2,0,1:T(8,128)(2,1)S(1)}, u32[]{:S(2)}) copy-start(bf16[128,2,64]{2,0,1:T(8,128)(2,1)S(1)} %get-tuple-element.13) | copy-start | bytes 98308
  77.2 2.0 copy-start.9
  161.3 3.8 copy-start.13
  161.3 3.9 copy-start.11
  171.9 142.7 %all-to-all-start.5 = ((bf16[64,20,1024]{2,1,0:T(8,128)(2,1)}), bf16[64,20,1024]{2,1,0:T(8,128)(2,1)}, u32[]{:S(2)}, u32[]{:S(2)}) async-start(bf16[64,20,1024]{2,1,0:T(8,128)(2,1)} %reshape.331), calls=%async_computation.5 | async-start | bytes 6291456 | tf_op jit(solution)/shard_map/all_to_all | solution.py:177
  181.2 137.1 %all-gather.7.cloned.1.call-start = ((), (), s32[]{:S(2)}) async-start(), calls=%async_computation.8 | async-start | bytes 1769472 | tf_op jit(solution)/shard_map/all_gather | solution.py:180
  181.8 142.0 %all-gather.11.cloned.1.call-start = ((), (), s32[]{:S(2)}) async-start(), calls=%async_computation.10 | async-start | bytes 1769472 | tf_op jit(solution)/shard_map/all_gather | solution.py:182
  182.4 141.4 %all-gather.9.cloned.1.call-start = ((), (), s32[]{:S(2)}) async-start(), calls=%async_computation.9 | async-start | bytes 1769472 | tf_op jit(solution)/shard_map/all_gather | solution.py:181
  339.0 8.0 %copy-start.12 = (f32[128,8]{0,1:T(8,128)S(1)}, f32[128,8]{0,1:T(8,128)}, u32[]{:S(2)}) copy-start(f32[128,8]{0,1:T(8,128)} %param.28) | copy-start | bytes 12292
  339.0 8.1 %copy-start.6 = (s32[128,64]{0,1:T(8,128)S(1)}, s32[128,64]{0,1:T(8,128)}, u32[]{:S(2)}) copy-start(s32[128,64]{0,1:T(8,128)} %copy-done.5) | copy-start | bytes 98308
  339.0 8.1 %copy-start.10 = (s32[128,8]{0,1:T(8,128)S(1)}, s32[128,8]{0,1:T(8,128)}, u32[]{:S(2)}) copy-start(s32[128,8]{0,1:T(8,128)} %param.27) | copy-start | bytes 12292
  339.0 143.5 %all-to-all-start.6 = ((bf16[64,20,1024]{2,1,0:T(8,128)(2,1)}), bf16[64,20,1024]{2,1,0:T(8,128)(2,1)}, u32[]{:S(2)}, u32[]{:S(2)}) async-start(bf16[64,20,1024]{2,1,0:T(8,128)(2,1)} %reshape.333), calls=%async_computation.6 | async-start | bytes 6291456 | tf_op jit(solution)/shard_map/all_to_all | solution.py:187
  (3 other events, 2.2 us)
Sparse Core Ops, SparseCore 0:
  11.1 150.1 all-gather.4
Sparse Core Ops, SparseCore 1:
  183.8 32.6 all-gather.6
  218.4 32.1 all-gather.10
  252.6 32.1 all-gather.8
where the time goes:
time: 509 us; the launch traced here: 508 us
  waiting for transfers between devices  379 us (74%)
  local copies, waits for them, and re-layouts  45.3 us (9%)
  starting transfers between devices  37.1 us (7%)
  matrix products  21.2 us (4%)
  between operations  15.5 us (3%)
  other arithmetic  10.6 us (2%)
    all_to_all x1, waiting for transfers between devices, local(): lax.all_to_all(out_slots, 'expert', split_axis=0, concat_axis=0, tiled=True)  135 us
    all_to_all x1, waiting for transfers between devices, local(): lax.all_to_all(outgoing, 'expert', split_axis=0, concat_axis=0, tiled=True)  132 us
    all_gather x1, waiting for transfers between devices, project_heads(): lax.all_gather(output_weight, 'expert', axis=0, tiled=True)  81.6 us
    all_to_all x1, waiting for transfers between devices, local(): lax.all_to_all(query_rows[source_rows].reshape(owner_total, capacity, -1)...  11.9 us
    gather x8, local copies, waits for them, and re-layouts, local(): flat_back[copy_index[:, route_slot]].astype(jnp.float32)  11.8 us
  transfers between devices with their start and end apart: 11, of which 7 were waited for; matrix products, arithmetic and copies ran while one was open for 6% of the time, Pallas kernels for 0%

commit v1 on v0

--- a/solution.py
+++ b/solution.py
@@ -63,7 +63,10 @@
 def project_heads(attended, output_weight):
     return jnp.dot(
         attended,
-        lax.all_gather(output_weight, "expert", axis=0, tiled=True),
+        jnp.concatenate(
+            lax.all_to_all(jnp.stack([output_weight] * lax.axis_size("expert")), "expert", 0, 0),
+            axis=0,
+        ),
         preferred_element_type=jnp.float32,
     )
 

time: 509 us -> 636 us (1.25)
  waiting for transfers between devices: 379 us -> 477 us
  blocking collectives: 0 us -> 15.6 us
  starting transfers between devices: 37.1 us -> 49.5 us
    all_to_all x1, waiting for transfers between devices: 11.9 us -> 174 us  [project_heads(): lax.all_to_all(jnp.stack([output_weight] * lax.axis_size('expert')), 'exp...]
    all_gather x1 -> x0, waiting for transfers between devices: 81.6 us -> none  [project_heads(): lax.all_gather(output_weight, 'expert', axis=0, tiled=True)]
    all_to_all x0 -> x1, blocking collectives: none -> 15.6 us  [local(): lax.all_to_all(query_rows[source_rows].reshape(owner_total, capacity, -1)...]
    all_to_all x1, starting transfers between devices: 3.55 us -> 18.7 us  [project_heads(): lax.all_to_all(jnp.stack([output_weight] * lax.axis_size('expert')), 'exp...]
    all_to_all x1, waiting for transfers between devices: 132 us -> 140 us  [local(): lax.all_to_all(outgoing, 'expert', split_axis=0, concat_axis=0, tiled=True)]
    all_to_all x1, waiting for transfers between devices: 135 us -> 143 us  [local(): lax.all_to_all(out_slots, 'expert', split_axis=0, concat_axis=0, tiled=True)]
  transfers between devices with their start and end apart: 11 -> 10, of which waited for: 7 -> 7; matrix products, arithmetic and copies ran while one was open for 6% -> 5% of each run, Pallas kernels for 0% -> 0%
where the time goes in v1:
time: 636 us; the launch traced here: 635 us
  waiting for transfers between devices  477 us (75%)
  starting transfers between devices  49.5 us (8%)
  local copies, waits for them, and re-layouts  48.4 us (8%)
  matrix products  21.2 us (3%)
  blocking collectives  15.6 us (2%)
  between operations  13.6 us (2%)
  other arithmetic  10 us (2%)
    all_to_all x1, waiting for transfers between devices, project_heads(): lax.all_to_all(jnp.stack([output_weight] * lax.axis_size('expert')), 'exp...  174 us
    all_to_all x1, waiting for transfers between devices, local(): lax.all_to_all(out_slots, 'expert', split_axis=0, concat_axis=0, tiled=True)  143 us
    all_to_all x1, waiting for transfers between devices, local(): lax.all_to_all(outgoing, 'expert', split_axis=0, concat_axis=0, tiled=True)  140 us
    all_to_all x1, starting transfers between devices, project_heads(): lax.all_to_all(jnp.stack([output_weight] * lax.axis_size('expert')), 'exp...  18.7 us
    all_to_all x1, blocking collectives, local(): lax.all_to_all(query_rows[source_rows].reshape(owner_total, capacity, -1)...  15.6 us
  transfers between devices with their start and end apart: 10, of which 7 were waited for; matrix products, arithmetic and copies ran while one was open for 5% of the time, Pallas kernels for 0%

profile of v1, /device:TPU:32, one launch (start us, length us, event | category | flops | bytes accessed | tf_op | source)
XLA Modules:
  0.0 634.8 jit_solution(3405658623122743623)
XLA Ops:
  9.6 4.3 all-to-all-start.1
  16.4 2.7 all-to-all-done.1
  19.1 3.4 all-to-all-start.3
  24.9 3.4 all-to-all-done.3
  28.2 3.4 all-to-all-start.2
  33.4 4.0 all-to-all-done.2
  37.3 3.5 all-to-all-start
  41.9 7.7 %all-to-all-done = bf16[8,24,1024]{2,1,0:T(8,128)(2,1)S(1)} async-done(((bf16[8,24,1024]{2,1,0:T(8,128)(2,1)}), bf16[8,24,1024]{2,1,0:T(8,128)(2,1)S(1)}, u32[]{:S(2)}, u32[]{:S(2)}) %all-to-all-start) | async-done | bytes 393248 | tf_op jit(solution)/shard_map/all_to_all | solution.py:147
  49.6 15.6 %all_to_all.41 = bf16[8,24,2048]{2,1,0:T(8,128)(2,1)S(1)} all-to-all(bf16[8,24,2048]{2,1,0:T(8,128)(2,1)S(1)} %bitcast.109), channel_id=1, replica_groups=mesh['dp'=8,'expert'=64] {'dp'}, dimensions={0} | all-to-all | bytes 1572864 | tf_op jit(solution)/shard_map/all_to_all | solution.py:126
  65.2 2.5 stack.2
  67.7 18.7 %all-to-all-start.5 = ((bf16[64,32,1024]{2,1,0:T(8,128)(2,1)}), bf16[64,32,1024]{2,1,0:T(8,128)(2,1)}, u32[]{:S(2)}, u32[]{:S(2)}) async-start(bf16[64,32,1024]{2,1,0:T(8,128)(2,1)} %stack.2), calls=%async_computation.5 | async-start | bytes 8388608 | tf_op jit(solution)/shard_map/all_to_all | solution.py:67
  99.6 173.7 %all-to-all-done.5 = bf16[64,32,1024]{2,1,0:T(8,128)(2,1)} async-done(((bf16[64,32,1024]{2,1,0:T(8,128)(2,1)}), bf16[64,32,1024]{2,1,0:T(8,128)(2,1)}, u32[]{:S(2)}, u32[]{:S(2)}) %all-to-all-start.5) | async-done | bytes 4194336 | tf_op jit(solution)/shard_map/all_to_all | solution.py:67
  273.3 3.0 multiply_reduce_fusion.1
  277.3 4.3 gather_fusion.8
  284.0 8.3 %all-to-all-start.6 = ((bf16[64,20,1024]{2,1,0:T(8,128)(2,1)}), bf16[64,20,1024]{2,1,0:T(8,128)(2,1)}, u32[]{:S(2)}, u32[]{:S(2)}) async-start(bf16[64,20,1024]{2,1,0:T(8,128)(2,1)} %reshape.337), calls=%async_computation.6 | async-start | bytes 6291456 | tf_op jit(solution)/shard_map/all_to_all | solution.py:180
  294.5 140.4 %all-to-all-done.6 = bf16[64,20,1024]{2,1,0:T(8,128)(2,1)} async-done(((bf16[64,20,1024]{2,1,0:T(8,128)(2,1)}), bf16[64,20,1024]{2,1,0:T(8,128)(2,1)}, u32[]{:S(2)}, u32[]{:S(2)}) %all-to-all-start.6) | async-done | bytes 2621472 | tf_op jit(solution)/shard_map/all_to_all | solution.py:180
  434.9 3.6 reshape.338
  438.6 5.5 fusion.4
  444.1 10.0 %convolution_convert_fusion = bf16[1280,1024]{1,0:T(8,128)(2,1)} fusion(bf16[1,768,1024]{2,1,0:T(8,128)(2,1)} %all-gather.8.cloned.1.call-done, bf16[1280,1024]{1,0:T(8,128)(2,1)S(1)} %reshape.338, f32[1280,768]{1,0:T(8,128)} %fusion.4, bf16[1,768,1024]{2,1,0:T(8,128)(2,1)} %all-gather.6.cloned.1.call-done), kind=kOutput, calls=%fused_computation.19 | convolution fusion | flops 4033740800 | bytes 12320768 | tf_op jit(solution)/shard_map/dot_general | solution.py:79
  454.1 5.2 reshape.339
  459.3 7.9 %all-to-all-start.7 = ((bf16[64,20,1024]{2,1,0:T(8,128)(2,1)}), bf16[64,20,1024]{2,1,0:T(8,128)(2,1)}, u32[]{:S(2)}, u32[]{:S(2)}) async-start(bf16[64,20,1024]{2,1,0:T(8,128)(2,1)} %reshape.339), calls=%async_computation.7 | async-start | bytes 6291456 | tf_op jit(solution)/shard_map/all_to_all | solution.py:190
  467.4 142.7 %all-to-all-done.7 = bf16[64,20,1024]{2,1,0:T(8,128)(2,1)} async-done(((bf16[64,20,1024]{2,1,0:T(8,128)(2,1)}), bf16[64,20,1024]{2,1,0:T(8,128)(2,1)}, u32[]{:S(2)}, u32[]{:S(2)}) %all-to-all-start.7) | async-done | bytes 2621472 | tf_op jit(solution)/shard_map/all_to_all | solution.py:190
  610.1 3.6 reshape.340
  625.5 2.8 add_convert_fusion.1
  (116 shorter events, 41.2 us)
Async XLA Ops:
  6.5 34.2 %copy-start = (bf16[128,2048]{1,0:T(8,128)(2,1)S(1)}, bf16[128,2048]{1,0:T(8,128)(2,1)}, u32[]{:S(2)}) copy-start(bf16[128,2048]{1,0:T(8,128)(2,1)} %param.16) | copy-start | bytes 1572868
  6.5 25.1 %copy-start.1 = (bf16[128,1024]{1,0:T(8,128)(2,1)S(1)}, bf16[128,1024]{1,0:T(8,128)(2,1)}, u32[]{:S(2)}) copy-start(bf16[128,1024]{1,0:T(8,128)(2,1)} %param.19) | copy-start | bytes 786436
  9.6 9.5 %all-to-all-start.1 = ((s32[8,1,24]{2,1,0:T(1,128)}), s32[8,1,24]{2,1,0:T(1,128)S(1)}, u32[]{:S(2)}, u32[]{:S(2)}) async-start(s32[8,1,24]{2,1,0:T(1,128)} %compare_select_fusion.1), calls=%async_computation.1 | async-start | bytes 8192 | tf_op jit(solution)/shard_map/all_to_all | solution.py:154
  19.1 9.1 %all-to-all-start.3 = ((bf16[8,24,256]{2,1,0:T(8,128)(2,1)}), bf16[8,24,256]{2,1,0:T(8,128)(2,1)S(1)}, u32[]{:S(2)}, u32[]{:S(2)}) async-start(bf16[8,24,256]{2,1,0:T(8,128)(2,1)} %bitcast.14), calls=%async_computation.3 | async-start | bytes 196608 | tf_op jit(solution)/shard_map/all_to_all | solution.py:133
  28.2 9.1 %all-to-all-start.2 = ((bf16[8,24,256]{2,1,0:T(8,128)(2,1)}), bf16[8,24,256]{2,1,0:T(8,128)(2,1)S(1)}, u32[]{:S(2)}, u32[]{:S(2)}) async-start(bf16[8,24,256]{2,1,0:T(8,128)(2,1)} %bitcast.9), calls=%async_computation.2 | async-start | bytes 196608 | tf_op jit(solution)/shard_map/all_to_all | solution.py:140
  37.3 12.3 %all-to-all-start = ((bf16[8,24,1024]{2,1,0:T(8,128)(2,1)}), bf16[8,24,1024]{2,1,0:T(8,128)(2,1)S(1)}, u32[]{:S(2)}, u32[]{:S(2)}) async-start(bf16[8,24,1024]{2,1,0:T(8,128)(2,1)} %bitcast.3), calls=%async_computation | async-start | bytes 786432 | tf_op jit(solution)/shard_map/all_to_all | solution.py:147
  40.8 24.4 %copy-start.7 = (bf16[32,1024]{1,0:T(8,128)(2,1)S(1)}, bf16[32,1024]{1,0:T(8,128)(2,1)}, u32[]{:S(2)}) copy-start(bf16[32,1024]{1,0:T(8,128)(2,1)} %param.25) | copy-start | bytes 196612
  67.7 18.7 %copy-start.9 = (s32[128,8]{0,1:T(8,128)S(1)}, s32[128,8]{0,1:T(8,128)}, u32[]{:S(2)}) copy-start(s32[128,8]{0,1:T(8,128)} %param.27) | copy-start | bytes 12292
  67.7 25.4 %copy-start.14 = (f32[128]{0:T(128)S(1)}, f32[128]{0:T(128)}, u32[]{:S(2)}) copy-start(f32[128]{0:T(128)} %param.24) | copy-start | bytes 1540
  67.7 205.6 %all-to-all-start.5 = ((bf16[64,32,1024]{2,1,0:T(8,128)(2,1)}), bf16[64,32,1024]{2,1,0:T(8,128)(2,1)}, u32[]{:S(2)}, u32[]{:S(2)}) async-start(bf16[64,32,1024]{2,1,0:T(8,128)(2,1)} %stack.2), calls=%async_computation.5 | async-start | bytes 8388608 | tf_op jit(solution)/shard_map/all_to_all | solution.py:67
  93.3 3.9 copy-start.5
  93.3 3.9 copy-start.6
  95.1 0.8 copy-start.15
  97.1 2.0 copy-start.8
  273.3 3.8 copy-start.13
  273.3 4.0 copy-start.11
  284.0 151.0 %all-to-all-start.6 = ((bf16[64,20,1024]{2,1,0:T(8,128)(2,1)}), bf16[64,20,1024]{2,1,0:T(8,128)(2,1)}, u32[]{:S(2)}, u32[]{:S(2)}) async-start(bf16[64,20,1024]{2,1,0:T(8,128)(2,1)} %reshape.337), calls=%async_computation.6 | async-start | bytes 6291456 | tf_op jit(solution)/shard_map/all_to_all | solution.py:180
  292.3 146.3 %all-gather.4.cloned.1.call-start = ((), (), s32[]{:S(2)}) async-start(), calls=%async_computation.8 | async-start | bytes 1769472 | tf_op jit(solution)/shard_map/all_gather | solution.py:183
  293.0 151.1 %all-gather.6.cloned.1.call-start = ((), (), s32[]{:S(2)}) async-start(), calls=%async_computation.9 | async-start | bytes 1769472 | tf_op jit(solution)/shard_map/all_gather | solution.py:184
  293.8 150.4 %all-gather.8.cloned.1.call-start = ((), (), s32[]{:S(2)}) async-start(), calls=%async_computation.10 | async-start | bytes 1769472 | tf_op jit(solution)/shard_map/all_gather | solution.py:185
  459.3 7.9 %copy-start.12 = (f32[128,8]{0,1:T(8,128)S(1)}, f32[128,8]{0,1:T(8,128)}, u32[]{:S(2)}) copy-start(f32[128,8]{0,1:T(8,128)} %param.28) | copy-start | bytes 12292
  459.3 7.9 %copy-start.4 = (s32[128,64]{0,1:T(8,128)S(1)}, s32[128,64]{0,1:T(8,128)}, u32[]{:S(2)}) copy-start(s32[128,64]{0,1:T(8,128)} %copy-done.3) | copy-start | bytes 98308
  459.3 7.9 %copy-start.10 = (s32[128,8]{0,1:T(8,128)S(1)}, s32[128,8]{0,1:T(8,128)}, u32[]{:S(2)}) copy-start(s32[128,8]{0,1:T(8,128)} %param.27) | copy-start | bytes 12292
  459.3 150.7 %all-to-all-start.7 = ((bf16[64,20,1024]{2,1,0:T(8,128)(2,1)}), bf16[64,20,1024]{2,1,0:T(8,128)(2,1)}, u32[]{:S(2)}, u32[]{:S(2)}) async-start(bf16[64,20,1024]{2,1,0:T(8,128)(2,1)} %reshape.339), calls=%async_computation.7 | async-start | bytes 6291456 | tf_op jit(solution)/shard_map/all_to_all | solution.py:190
  (2 other events, 1.4 us)
Sparse Core Ops, SparseCore 0:
  295.2 30.9 all-gather.3
  328.3 32.2 all-gather.5
  362.7 32.2 all-gather.7
